TPU v7x, 512 devices: a whole 4x4x16 slice. The times are simulated.
512 devices in a mesh: row: 16 (over y, x_lo, core), col: 32 (over z, x_hi).
Axes of the slice: x: 4 (x_hi: 2, x_lo: 2; x = x_hi * 2 + x_lo), y: 4, z: 16, core: 2. Of those that a mesh axis runs over, the one named last changes fastest.
Arguments:
- velocity: bfloat16 [3, 512, 512, 512], P(None, 'row', 'col'), may hold values from -6 to 6
- wall_slope: bfloat16 [512, 512], replicated, may hold values from -0.25 to 0.25
- wall_diffusion: bfloat16 [512, 512], replicated, may hold values from -0.25 to 0.25
- span_slope: bfloat16 [512, 512], replicated, may hold values from -0.25 to 0.25
- span_diffusion: bfloat16 [512, 512], replicated, may hold values from -0.25 to 0.25
Outputs:
- tendency: bfloat16 [3, 512, 512, 512], P(None, 'row', 'col')
All inputs are finite; a program needn't handle non-finite values.
Results may differ from a plain program's by a relative error of at most 0.0051.
Values may be sent and summed in bfloat16 or wider, within the bound.
No kernel may reach another device: no remote copies, remote signals or barrier semaphores. Data moves between devices by JAX's collectives and lax.ppermute only.
A program may use at most 128 MiB of HBM per device.

v0:
```python
import jax
import jax.numpy as jnp
from jax import lax
from jax.sharding import PartitionSpec as P


def rate_of_change(speed_rate_change, molecular_smoothing, strip_sets, flow_speed_holder):
    spatial_rate_map = jnp.einsum(
        "ij,cjm->cim", speed_rate_change, strip_sets, preferred_element_type=jnp.float32
    )
    second_derivative = jnp.einsum(
        "ij,cjm->cim", molecular_smoothing, strip_sets, preferred_element_type=jnp.float32
    )
    tendency_term = (
        second_derivative
        - strip_sets[flow_speed_holder][None].astype(jnp.float32) * spatial_rate_map
    )
    return lax.optimization_barrier(tendency_term.astype(jnp.bfloat16))


def per_device(velocity, wall_slope, wall_diffusion, span_slope, span_diffusion):
    row_count = lax.axis_size("row")
    column_count = lax.axis_size("col")
    comps, wall_local, span_local, stream_len = velocity.shape
    wall_total = wall_local * row_count
    span_total = span_local * column_count
    stream_row = stream_len // row_count
    arranged = velocity.reshape(comps, wall_local, span_local, row_count, stream_row)
    arranged = arranged.transpose(0, 1, 3, 2, 4).reshape(
        comps, wall_local, row_count, span_local * stream_row
    )
    wall_lines = lax.all_to_all(arranged, "row", split_axis=2, concat_axis=1, tiled=True)
    wall_lines = wall_lines.reshape(comps, wall_total, span_local * stream_row)
    wall_term = rate_of_change(wall_slope, wall_diffusion, wall_lines, 1)
    wall_share = wall_total // column_count
    sectioned = wall_lines.reshape(comps, column_count, wall_share, span_local, stream_row)
    sectioned = sectioned.transpose(0, 3, 1, 2, 4).reshape(
        comps, span_local, column_count, wall_share * stream_row
    )
    span_lines = lax.all_to_all(sectioned, "col", split_axis=2, concat_axis=1, tiled=True)
    span_lines = span_lines.reshape(comps, span_total, wall_share * stream_row)
    crosswise_contribution = rate_of_change(span_slope, span_diffusion, span_lines, 2)
    returned = lax.all_to_all(
        crosswise_contribution.reshape(comps, column_count, span_local, wall_share * stream_row),
        "col",
        split_axis=1,
        concat_axis=1,
        tiled=True,
    )
    returned = returned.reshape(comps, column_count, span_local, wall_share, stream_row)
    returned = returned.transpose(0, 1, 3, 2, 4).reshape(comps, wall_total, span_local * stream_row)
    summed = (wall_term.astype(jnp.float32) + returned.astype(jnp.float32)).astype(jnp.bfloat16)
    homeward = lax.all_to_all(
        summed.reshape(comps, row_count, wall_local, span_local * stream_row),
        "row",
        split_axis=1,
        concat_axis=1,
        tiled=True,
    )
    homeward = homeward.reshape(comps, row_count, wall_local, span_local, stream_row)
    return homeward.transpose(0, 2, 3, 1, 4).reshape(comps, wall_local, span_local, stream_len)


def solution(mesh):
    in_specs = (P(None, "row", "col", None), P(), P(), P(), P())
    out_specs = P(None, "row", "col", None)
    return jax.shard_map(
        per_device, mesh=mesh, in_specs=in_specs, out_specs=out_specs, check_vma=False
    )
```

profile of v0, /device:TPU:1, one launch (start us, length us, event | category | flops | bytes accessed | tf_op | source)
XLA Modules:
  0.0 362.1 jit_solution(13260486315571483429)
XLA Ops:
  0.0 8.0 %reshape.56 = bf16[3,32,16,16,32]{4,3,2,1,0:T(8,128)(2,1)} reshape(bf16[3,32,16,512]{3,2,1,0:T(8,128)(2,1)} %param.5) | data formatting | bytes 3145728 | tf_op jit(solution)/shard_map/reshape | solution.py:28
  8.0 7.0 %copy.66 = bf16[3,32,16,16,32]{4,2,1,0,3:T(8,128)(2,1)} copy(bf16[3,32,16,16,32]{4,3,2,1,0:T(8,128)(2,1)} %reshape.56) | data formatting | bytes 3145728 | tf_op jit(solution)/shard_map/reshape | solution.py:28
  15.1 8.4 %reshape.57 = bf16[3,32,16,512]{3,1,0,2:T(8,128)(2,1)S(1)} reshape(bf16[3,32,16,16,32]{4,3,1,0,2:T(8,128)(2,1)} %bitcast.88) | data formatting | bytes 3145728 | tf_op jit(solution)/shard_map/reshape | solution.py:29
  23.5 30.3 %all_to_all.40 = bf16[3,32,16,512]{3,1,0,2:T(8,128)(2,1)S(1)} all-to-all(bf16[3,32,16,512]{3,1,0,2:T(8,128)(2,1)S(1)} %reshape.57), channel_id=1, replica_groups=mesh['row'=16,'col'=32] {'row'}, dimensions={2} | all-to-all | bytes 3145728 | tf_op jit(solution)/shard_map/all_to_all | solution.py:32
  53.8 5.4 %reshape_reshape.3 = bf16[3,32,16,16,32]{4,3,2,1,0:T(8,128)(2,1)} reshape(bf16[3,16,32,1,512]{4,2,1,0,3:T(8,128)(2,1)S(1)} %bitcast.84) | data formatting | bytes 3145728 | tf_op jit(solution)/shard_map/reshape;reshape | solution.py:36
  59.2 8.0 %copy.59 = bf16[3,16,32,16,32]{4,3,1,0,2:T(8,128)(2,1)} copy(bf16[3,16,32,16,32]{4,1,3,2,0:T(8,128)(2,1)} %bitcast.90) | data formatting | bytes 3145728 | tf_op jit(solution)/shard_map/reshape | solution.py:37
  67.3 9.3 %reshape.73 = bf16[3,16,32,512]{3,1,0,2:T(8,128)(2,1)} reshape(bf16[3,16,32,16,32]{4,3,1,0,2:T(8,128)(2,1)} %copy.59) | data formatting | bytes 3145728 | tf_op jit(solution)/shard_map/reshape | solution.py:37
  76.6 90.7 %all_to_all.41 = bf16[3,16,32,512]{3,1,0,2:T(8,128)(2,1)S(1)} all-to-all(bf16[3,16,32,512]{3,1,0,2:T(8,128)(2,1)} %reshape.73), channel_id=1, replica_groups=mesh['row'=16,'col'=32] {'col'}, dimensions={2} | all-to-all | bytes 3145728 | tf_op jit(solution)/shard_map/all_to_all | solution.py:40
  167.4 1.1 copy-done.2
  168.6 1.1 bitcast_convert_fusion
  169.7 1.6 copy.45
  171.3 2.6 fusion.5
  173.9 2.3 fusion.1
  176.2 2.6 copy.47
  178.8 2.7 copy.48
  181.5 6.8 %all-to-all-start.2 = ((bf16[3,32,16,512]{3,2,0,1:T(8,128)(2,1)}), bf16[3,32,16,512]{3,2,0,1:T(8,128)(2,1)}, u32[]{:S(2)}, u32[]{:S(2)}) async-start(bf16[3,32,16,512]{3,2,0,1:T(8,128)(2,1)} %copy.48), calls=%async_computation.2 | async-start | bytes 3145728 | tf_op jit(solution)/shard_map/all_to_all | solution.py:43
  188.3 1.1 bitcast_convert_fusion.1
  189.5 1.6 copy.39
  191.1 1.0 fusion.8
  192.2 2.4 fusion.3
  194.6 68.4 %all-to-all-done.2 = bf16[3,32,16,512]{3,2,0,1:T(8,128)(2,1)} async-done(((bf16[3,32,16,512]{3,2,0,1:T(8,128)(2,1)}), bf16[3,32,16,512]{3,2,0,1:T(8,128)(2,1)}, u32[]{:S(2)}, u32[]{:S(2)}) %all-to-all-start.2) | async-done | bytes 1572896 | tf_op jit(solution)/shard_map/all_to_all | solution.py:43
  263.0 3.5 copy.49
  266.5 8.5 %reshape.68 = f32[3,32,16,16,32]{4,3,2,1,0:T(8,128)} reshape(f32[3,32,16,512]{3,2,1,0:T(8,128)} %copy.49) | data formatting | bytes 6291456 | tf_op jit(solution)/shard_map/convert_element_type | solution.py:52
  275.1 15.1 %copy.50 = f32[3,32,16,16,32]{4,3,2,1,0:T(8,128)} copy(f32[3,32,16,16,32]{4,2,3,1,0:T(8,128)} %bitcast.83) | data formatting | bytes 6291456 | tf_op jit(solution)/shard_map/convert_element_type | solution.py:52
  290.1 9.9 %reshape.67 = f32[3,512,512]{2,1,0:T(8,128)} reshape(f32[3,32,16,16,32]{4,3,2,1,0:T(8,128)} %copy.50) | data formatting | bytes 6291456 | tf_op jit(solution)/shard_map/convert_element_type | solution.py:52
  300.1 3.7 %copy.51 = f32[3,512,512]{1,2,0:T(8,128)} copy(f32[3,512,512]{2,1,0:T(8,128)} %reshape.67) | data formatting | bytes 6291456 | tf_op jit(solution)/shard_map/convert_element_type | solution.py:52
  303.8 3.6 add_convert_fusion
  307.4 1.9 copy.52
  309.4 25.3 %all_to_all.42 = bf16[3,16,32,512]{3,2,0,1:T(8,128)(2,1)S(1)} all-to-all(bf16[3,16,32,512]{3,2,0,1:T(8,128)(2,1)S(1)} %copy.53), channel_id=1, replica_groups=mesh['row'=16,'col'=32] {'row'}, dimensions={1} | all-to-all | bytes 3145728 | tf_op jit(solution)/shard_map/all_to_all | solution.py:53
  334.7 5.4 %reshape.63 = bf16[3,16,32,16,32]{4,3,2,0,1:T(8,128)(2,1)} reshape(bf16[3,16,32,512]{3,2,0,1:T(8,128)(2,1)S(1)} %all_to_all.42) | data formatting | bytes 3145728 | tf_op jit(solution)/shard_map/reshape | solution.py:60
  340.1 12.7 %copy.54 = bf16[3,32,16,16,32]{4,3,2,1,0:T(8,128)(2,1)} copy(bf16[3,32,16,16,32]{4,2,1,0,3:T(8,128)(2,1)} %bitcast.89) | data formatting | bytes 3145728 | tf_op jit(solution)/shard_map/transpose | solution.py:61
  352.8 9.3 %reshape.64 = bf16[3,32,16,512]{3,2,1,0:T(8,128)(2,1)} reshape(bf16[3,32,16,16,32]{4,3,2,1,0:T(8,128)(2,1)} %copy.54) | data formatting | bytes 3145728 | tf_op jit(solution)/shard_map/reshape | solution.py:61
  (20 shorter events, 0.5 us)
Async XLA Ops:
  0.0 171.2 %copy-start = (bf16[512,512]{1,0:T(8,128)(2,1)S(1)}, bf16[512,512]{1,0:T(8,128)(2,1)}, u32[]{:S(2)}) copy-start(bf16[512,512]{1,0:T(8,128)(2,1)} %param.9) | copy-start | bytes 1572868
  167.4 1.1 copy-start.2
  171.3 2.6 copy-start.3
  171.3 2.6 copy-start.6
  181.5 81.5 %all-to-all-start.2 = ((bf16[3,32,16,512]{3,2,0,1:T(8,128)(2,1)}), bf16[3,32,16,512]{3,2,0,1:T(8,128)(2,1)}, u32[]{:S(2)}, u32[]{:S(2)}) async-start(bf16[3,32,16,512]{3,2,0,1:T(8,128)(2,1)} %copy.48), calls=%async_computation.2 | async-start | bytes 3145728 | tf_op jit(solution)/shard_map/all_to_all | solution.py:43
  189.5 1.6 copy-start.5
  191.1 1.1 copy-start.7
  300.1 3.7 %copy-start.4 = (bf16[3,512,512]{1,2,0:T(8,128)(2,1)S(1)}, bf16[3,512,512]{1,2,0:T(8,128)(2,1)}, u32[]{:S(2)}) copy-start(bf16[3,512,512]{1,2,0:T(8,128)(2,1)} %fusion.3) | copy-start | bytes 4718596
  352.8 9.4 %copy-start.1 = (bf16[512,512]{1,0:T(8,128)(2,1)S(1)}, bf16[512,512]{1,0:T(8,128)(2,1)}, u32[]{:S(2)}) copy-start(bf16[512,512]{1,0:T(8,128)(2,1)} %param.9) | copy-start | bytes 1572868
where the time goes:
time: 366 us; the launch traced here: 362 us
  blocking collectives  146 us (40%)
  local copies, waits for them, and re-layouts  126 us (34%)
  waiting for transfers between devices  68.4 us (19%)
  matrix products  8.36 us (2%)
  starting transfers between devices  6.81 us (2%)
  other arithmetic  5.82 us (2%)
    all_to_all x1, blocking collectives, per_device(): lax.all_to_all(sectioned, 'col', split_axis=2, concat_axis=1, tiled=True)  90.7 us
    all_to_all x1, waiting for transfers between devices, per_device(): lax.all_to_all(crosswise_contribution.reshape(comps, column_count, span_l...  68.4 us
    convert_element_type x5, local copies, waits for them, and re-layouts, per_device(): returned.astype(jnp.float32)  40.8 us
    all_to_all x1, blocking collectives, per_device(): lax.all_to_all(arranged, 'row', split_axis=2, concat_axis=1, tiled=True)  30.3 us
    all_to_all x1, blocking collectives, per_device(): lax.all_to_all(summed.reshape(comps, row_count, wall_local, span_local *...  25.3 us
    reshape x2, local copies, waits for them, and re-layouts, per_device(): sectioned.transpose(0, 3, 1, 2, 4)  17.3 us
    reshape x2, local copies, waits for them, and re-layouts, per_device(): velocity.reshape(comps, wall_local, span_local, row_count, stream_row)  15.1 us
    transpose x1, local copies, waits for them, and re-layouts, per_device(): homeward.transpose(0, 2, 3, 1, 4)  12.7 us
  transfers between devices with their start and end apart: 1, of which 1 were waited for; matrix products, arithmetic and copies ran while one was open for 2% of the time, Pallas kernels for 0%

commit v1 on v0

v1 whole, which is shorter than its diff:
```python
import jax
import jax.numpy as jnp
from jax import lax
from jax.sharding import PartitionSpec as P


def rate_of_change(slope, diffusion, lines, carrier):
    gradient = jnp.einsum("ij,cjm->cim", slope, lines, preferred_element_type=jnp.float32)
    curvature = jnp.einsum("ij,cjm->cim", diffusion, lines, preferred_element_type=jnp.float32)
    term = curvature - carrier[None].astype(jnp.float32) * gradient
    return term.astype(jnp.bfloat16)


def per_device(velocity, wall_slope, wall_diffusion, span_slope, span_diffusion):
    row_count = lax.axis_size("row")
    column_count = lax.axis_size("col")
    comps, wall_local, span_local, stream_len = velocity.shape
    wall_total = wall_local * row_count
    span_total = span_local * column_count
    span_share = span_local // row_count
    wall_share = wall_local // column_count

    wall_lines = lax.all_to_all(velocity, "row", split_axis=2, concat_axis=1, tiled=True)
    wall_flat = wall_lines.reshape(comps, wall_total, span_share * stream_len)
    wall_term = rate_of_change(wall_slope, wall_diffusion, wall_flat, wall_flat[1])
    wall_back = lax.all_to_all(
        wall_term.reshape(comps, wall_total, span_share, stream_len),
        "row", split_axis=1, concat_axis=2, tiled=True,
    )

    span_lines = lax.all_to_all(velocity, "col", split_axis=1, concat_axis=2, tiled=True)
    span_flat = span_lines.reshape(comps, wall_share, span_total, stream_len)
    span_terms = []
    for w in range(wall_share):
        block = span_flat[:, w]
        span_terms.append(rate_of_change(span_slope, span_diffusion, block, block[2]))
    span_term = jnp.stack(span_terms, axis=1)
    span_back = lax.all_to_all(span_term, "col", split_axis=2, concat_axis=1, tiled=True)

    summed = wall_back.astype(jnp.float32) + span_back.astype(jnp.float32)
    return summed.astype(jnp.bfloat16)


def solution(mesh):
    in_specs = (P(None, "row", "col", None), P(), P(), P(), P())
    out_specs = P(None, "row", "col", None)
    return jax.shard_map(
        per_device, mesh=mesh, in_specs=in_specs, out_specs=out_specs, check_vma=False
    )
```

time: 366 us -> 270 us (0.74)
  blocking collectives: 146 us -> 0 us
  waiting for transfers between devices: 68.4 us -> 190 us
  local copies, waits for them, and re-layouts: 126 us -> 28.6 us
  starting transfers between devices: 6.81 us -> 37 us
    all_to_all x3 -> x0, blocking collectives: 146 us -> none  [the longest x1 90.7 us: per_device(): lax.all_to_all(sectioned, 'col', split_axis=2, concat_axis=1, tiled=True)]
    all_to_all x1 -> x4, waiting for transfers between devices: 68.4 us -> 190 us  [the longest x1 94.5 us: per_device(): lax.all_to_all(span_term, 'col', split_axis=2, concat_axis=1, tiled=True)]
    reshape x9 -> x1, local copies, waits for them, and re-layouts: 58.3 us -> 4.39 us  [per_device(): wall_term.reshape(comps, wall_total, span_share, stream_len)]
    convert_element_type x8 -> x3, local copies, waits for them, and re-layouts: 45.9 us -> 6.11 us  [the longest x2 4.1 us: rate_of_change(): term = curvature - carrier[None].astype(jnp.float32) * gradient]
    all_to_all x1 -> x4, starting transfers between devices: 6.81 us -> 37 us  [the longest x1 13.3 us: per_device(): lax.all_to_all(velocity, 'col', split_axis=1, concat_axis=2, tiled=True)]
    transpose x1 -> x0, local copies, waits for them, and re-layouts: 12.7 us -> none  [per_device(): homeward.transpose(0, 2, 3, 1, 4)]
    all_to_all x2 -> x4, local copies, waits for them, and re-layouts: 0.25 us -> 6.58 us  [the longest x1 1.97 us: per_device(): lax.all_to_all(span_term, 'col', split_axis=2, concat_axis=1, tiled=True)]
    unnamed x16, local copies, waits for them, and re-layouts: 1.17 us -> 6.03 us
  transfers between devices with their start and end apart: 1 -> 4, of which waited for: 1 -> 4; matrix products, arithmetic and copies ran while one was open for 2% -> 11% of each run, Pallas kernels for 0% -> 0%
where the time goes in v1:
time: 270 us; the launch traced here: 267 us
  waiting for transfers between devices  190 us (70%)
  starting transfers between devices  37 us (14%)
  local copies, waits for them, and re-layouts  28.6 us (11%)
  matrix products  6.65 us (2%)
  other arithmetic  4.85 us (2%)
    all_to_all x1, waiting for transfers between devices, per_device(): lax.all_to_all(span_term, 'col', split_axis=2, concat_axis=1, tiled=True)  94.5 us
    all_to_all x1, waiting for transfers between devices, per_device(): lax.all_to_all(velocity, 'col', split_axis=1, concat_axis=2, tiled=True)  62.6 us
    all_to_all x1, waiting for transfers between devices, per_device(): lax.all_to_all(velocity, 'row', split_axis=2, concat_axis=1, tiled=True)  20.2 us
    all_to_all x1, starting transfers between devices, per_device(): lax.all_to_all(velocity, 'col', split_axis=1, concat_axis=2, tiled=True)  13.3 us
    all_to_all x1, waiting for transfers between devices, per_device(): lax.all_to_all(wall_term.reshape(comps, wall_total, span_share, stream_le...  12.7 us
    all_to_all x1, starting transfers between devices, per_device(): lax.all_to_all(velocity, 'row', split_axis=2, concat_axis=1, tiled=True)  11.1 us
    all_to_all x1, starting transfers between devices, per_device(): lax.all_to_all(span_term, 'col', split_axis=2, concat_axis=1, tiled=True)  7.37 us
    unnamed x16, local copies, waits for them, and re-layouts  6.03 us
  transfers between devices with their start and end apart: 4, of which 4 were waited for; matrix products, arithmetic and copies ran while one was open for 11% of the time, Pallas kernels for 0%

profile of v1, /device:TPU:1, one launch (start us, length us, event | category | flops | bytes accessed | tf_op | source)
XLA Modules:
  0.0 267.4 jit_solution(3634852275575527685)
XLA Ops:
  0.0 3.5 %copy.22 = bf16[3,32,16,512]{3,1,0,2:T(8,128)(2,1)} copy(bf16[3,32,16,512]{3,2,1,0:T(8,128)(2,1)} %param.5) | data formatting | bytes 3145728 | tf_op args[0]
  3.5 11.1 %all-to-all-start = ((bf16[3,32,16,512]{3,1,0,2:T(8,128)(2,1)}), bf16[3,32,16,512]{3,1,0,2:T(8,128)(2,1)}, u32[]{:S(2)}, u32[]{:S(2)}) async-start(bf16[3,32,16,512]{3,1,0,2:T(8,128)(2,1)} %copy.22), calls=%async_computation | async-start | bytes 3145728 | tf_op jit(solution)/shard_map/all_to_all | solution.py:23
  14.6 1.3 copy.29
  15.9 20.2 %all-to-all-done = bf16[3,32,16,512]{3,1,0,2:T(8,128)(2,1)} async-done(((bf16[3,32,16,512]{3,1,0,2:T(8,128)(2,1)}), bf16[3,32,16,512]{3,1,0,2:T(8,128)(2,1)}, u32[]{:S(2)}, u32[]{:S(2)}) %all-to-all-start) | async-done | bytes 1572896 | tf_op jit(solution)/shard_map/all_to_all | solution.py:23
  36.1 13.3 %all-to-all-start.2 = ((bf16[3,32,16,512]{3,2,0,1:T(8,128)(2,1)}), bf16[3,32,16,512]{3,2,0,1:T(8,128)(2,1)}, u32[]{:S(2)}, u32[]{:S(2)}) async-start(bf16[3,32,16,512]{3,2,0,1:T(8,128)(2,1)} %copy.29), calls=%async_computation.2 | async-start | bytes 3145728 | tf_op jit(solution)/shard_map/all_to_all | solution.py:31
  49.4 1.5 copy.45
  51.0 1.1 bitcast_convert_fusion.1
  52.1 1.6 copy.25
  53.7 0.0 copy-start.5
  53.7 1.0 fusion.11
  54.8 2.3 fusion.5
  57.1 4.4 %copy.27 = bf16[3,512,1,512]{3,0,2,1:T(4,128)(2,1)} copy(bf16[3,512,1,512]{1,3,0,2:T(8,128)(2,1)} %fusion.5) | data formatting | bytes 3145728 | tf_op jit(solution)/shard_map/reshape | solution.py:27
  61.5 62.6 %all-to-all-done.2 = bf16[3,32,16,512]{3,2,0,1:T(8,128)(2,1)} async-done(((bf16[3,32,16,512]{3,2,0,1:T(8,128)(2,1)}), bf16[3,32,16,512]{3,2,0,1:T(8,128)(2,1)}, u32[]{:S(2)}, u32[]{:S(2)}) %all-to-all-start.2) | async-done | bytes 1572896 | tf_op jit(solution)/shard_map/all_to_all | solution.py:31
  124.1 5.3 %all-to-all-start.1 = ((bf16[3,512,1,512]{3,0,2,1:T(4,128)(2,1)}), bf16[3,512,1,512]{3,0,2,1:T(4,128)(2,1)S(1)}, u32[]{:S(2)}, u32[]{:S(2)}) async-start(bf16[3,512,1,512]{3,0,2,1:T(4,128)(2,1)} %copy.27), calls=%async_computation.1 | async-start | bytes 4194304 | tf_op jit(solution)/shard_map/all_to_all | solution.py:26
  129.4 1.1 slice.11
  130.5 1.1 bitcast_convert_fusion
  131.6 2.5 copy.32
  134.1 1.6 copy.30
  135.8 1.0 fusion.8
  136.8 0.2 copy-done.3
  137.0 0.1 copy-done.6
  137.1 2.2 fusion.6
  139.3 4.4 %copy.34 = bf16[3,1,512,512]{3,0,1,2:T(4,128)(2,1)} copy(bf16[3,1,512,512]{2,3,0,1:T(8,128)(2,1)} %fusion.6) | data formatting | bytes 3145728 | tf_op jit(solution)/shard_map/stack | solution.py:37
  143.7 12.7 %all-to-all-done.1 = bf16[3,512,1,512]{3,0,2,1:T(4,128)(2,1)S(1)} async-done(((bf16[3,512,1,512]{3,0,2,1:T(4,128)(2,1)}), bf16[3,512,1,512]{3,0,2,1:T(4,128)(2,1)S(1)}, u32[]{:S(2)}, u32[]{:S(2)}) %all-to-all-start.1) | async-done | bytes 1572896 | tf_op jit(solution)/shard_map/all_to_all | solution.py:26
  156.4 7.4 %all-to-all-start.3 = ((bf16[3,1,512,512]{3,0,1,2:T(4,128)(2,1)}), bf16[3,1,512,512]{3,0,1,2:T(4,128)(2,1)}, u32[]{:S(2)}, u32[]{:S(2)}) async-start(bf16[3,1,512,512]{3,0,1,2:T(4,128)(2,1)} %copy.34), calls=%async_computation.3 | async-start | bytes 4194304 | tf_op jit(solution)/shard_map/all_to_all | solution.py:38
  163.8 1.5 copy.28
  165.3 94.5 %all-to-all-done.3 = bf16[3,1,512,512]{3,0,1,2:T(4,128)(2,1)} async-done(((bf16[3,1,512,512]{3,0,1,2:T(4,128)(2,1)}), bf16[3,1,512,512]{3,0,1,2:T(4,128)(2,1)}, u32[]{:S(2)}, u32[]{:S(2)}) %all-to-all-start.3) | async-done | bytes 1572896 | tf_op jit(solution)/shard_map/all_to_all | solution.py:38
  259.9 2.0 copy.35
  261.8 0.4 convert.9
  262.3 0.9 copy-done.2
  263.2 2.1 fusion
  265.4 2.0 copy.37
  (11 shorter events, 0.1 us)
Async XLA Ops:
  0.0 53.7 %copy-start = (bf16[512,512]{1,0:T(8,128)(2,1)S(1)}, bf16[512,512]{1,0:T(8,128)(2,1)}, u32[]{:S(2)}) copy-start(bf16[512,512]{1,0:T(8,128)(2,1)} %param.7) | copy-start | bytes 1572868
  3.5 11.1 %copy-start.1 = (bf16[3,32,16,512]{3,2,1,0:T(8,128)(2,1)S(1)}, bf16[3,32,16,512]{3,2,1,0:T(8,128)(2,1)}, u32[]{:S(2)}) copy-start(bf16[3,32,16,512]{3,2,1,0:T(8,128)(2,1)} %param.5) | copy-start | bytes 4718596
  3.5 32.6 %all-to-all-start = ((bf16[3,32,16,512]{3,1,0,2:T(8,128)(2,1)}), bf16[3,32,16,512]{3,1,0,2:T(8,128)(2,1)}, u32[]{:S(2)}, u32[]{:S(2)}) async-start(bf16[3,32,16,512]{3,1,0,2:T(8,128)(2,1)} %copy.22), calls=%async_computation | async-start | bytes 3145728 | tf_op jit(solution)/shard_map/all_to_all | solution.py:23
  36.1 88.0 %all-to-all-start.2 = ((bf16[3,32,16,512]{3,2,0,1:T(8,128)(2,1)}), bf16[3,32,16,512]{3,2,0,1:T(8,128)(2,1)}, u32[]{:S(2)}, u32[]{:S(2)}) async-start(bf16[3,32,16,512]{3,2,0,1:T(8,128)(2,1)} %copy.29), calls=%async_computation.2 | async-start | bytes 3145728 | tf_op jit(solution)/shard_map/all_to_all | solution.py:31
  53.7 1.1 copy-start.5
  124.1 32.3 %all-to-all-start.1 = ((bf16[3,512,1,512]{3,0,2,1:T(4,128)(2,1)}), bf16[3,512,1,512]{3,0,2,1:T(4,128)(2,1)S(1)}, u32[]{:S(2)}, u32[]{:S(2)}) async-start(bf16[3,512,1,512]{3,0,2,1:T(4,128)(2,1)} %copy.27), calls=%async_computation.1 | async-start | bytes 4194304 | tf_op jit(solution)/shard_map/all_to_all | solution.py:26
  134.1 1.6 copy-start.4
  135.7 1.2 copy-start.3
  135.8 1.3 copy-start.6
  156.4 103.4 %all-to-all-start.3 = ((bf16[3,1,512,512]{3,0,1,2:T(4,128)(2,1)}), bf16[3,1,512,512]{3,0,1,2:T(4,128)(2,1)}, u32[]{:S(2)}, u32[]{:S(2)}) async-start(bf16[3,1,512,512]{3,0,1,2:T(4,128)(2,1)} %copy.34), calls=%async_computation.3 | async-start | bytes 4194304 | tf_op jit(solution)/shard_map/all_to_all | solution.py:38
  261.8 1.4 copy-start.2

commit v2 on v1

v2 whole, which is shorter than its diff:
```python
import jax
import jax.numpy as jnp
from jax import lax
from jax.sharding import PartitionSpec as P


def per_device(velocity, wall_slope, wall_diffusion, span_slope, span_diffusion):
    row_count = lax.axis_size("row")
    column_count = lax.axis_size("col")
    comps, wall_local, span_local, stream_len = velocity.shape
    wall_total = wall_local * row_count
    span_total = span_local * column_count
    devices = row_count * column_count
    stream_share = stream_len // devices

    outgoing = velocity.reshape(comps, wall_local, span_local, devices, stream_share)
    outgoing = outgoing.transpose(3, 0, 1, 2, 4)
    planes = lax.all_to_all(outgoing, ("row", "col"), split_axis=0, concat_axis=0, tiled=True)
    planes = planes.reshape(row_count, column_count, comps, wall_local, span_local, stream_share)
    planes = planes.transpose(2, 5, 0, 3, 1, 4).reshape(comps, stream_share, wall_total, span_total)

    f32 = jnp.float32
    wall_gradient = jnp.einsum("ij,cxjz->cxiz", wall_slope, planes, preferred_element_type=f32)
    wall_curvature = jnp.einsum("ij,cxjz->cxiz", wall_diffusion, planes, preferred_element_type=f32)
    wall_term = (wall_curvature - planes[1][None].astype(f32) * wall_gradient).astype(jnp.bfloat16)
    span_gradient = jnp.einsum("ij,cxyj->cxyi", span_slope, planes, preferred_element_type=f32)
    span_curvature = jnp.einsum("ij,cxyj->cxyi", span_diffusion, planes, preferred_element_type=f32)
    span_term = (span_curvature - planes[2][None].astype(f32) * span_gradient).astype(jnp.bfloat16)
    summed = (wall_term.astype(f32) + span_term.astype(f32)).astype(jnp.bfloat16)

    homeward = summed.reshape(comps, stream_share, row_count, wall_local, column_count, span_local)
    homeward = homeward.transpose(2, 4, 0, 3, 5, 1).reshape(devices, comps, wall_local, span_local, stream_share)
    back = lax.all_to_all(homeward, ("row", "col"), split_axis=0, concat_axis=0, tiled=True)
    return back.transpose(1, 2, 3, 0, 4).reshape(comps, wall_local, span_local, stream_len)


def solution(mesh):
    in_specs = (P(None, "row", "col", None), P(), P(), P(), P())
    out_specs = P(None, "row", "col", None)
    return jax.shard_map(
        per_device, mesh=mesh, in_specs=in_specs, out_specs=out_specs, check_vma=False
    )
```

time: 270 us -> 317 us (1.17)
  blocking collectives: 0 us -> 192 us
  waiting for transfers between devices: 190 us -> 0 us
  local copies, waits for them, and re-layouts: 28.6 us -> 111 us
  starting transfers between devices: 37 us -> 0 us
    all_to_all x0 -> x2, blocking collectives: none -> 192 us  [the longest x1 104 us: per_device(): lax.all_to_all(outgoing, ('row', 'col'), split_axis=0, concat_axis=0, til...]
    all_to_all x4 -> x0, waiting for transfers between devices: 190 us -> none  [the longest x1 94.5 us: per_device(): lax.all_to_all(span_term, 'col', split_axis=2, concat_axis=1, tiled=True)]
    unnamed x16 -> x18, local copies, waits for them, and re-layouts: 6.03 us -> 52.1 us
    reshape x1 -> x5, local copies, waits for them, and re-layouts: 4.39 us -> 44 us  [the longest x2 14.9 us: per_device(): back.transpose(1, 2, 3, 0, 4)]
    all_to_all x4 -> x0, starting transfers between devices: 37 us -> none  [the longest x1 13.3 us: per_device(): lax.all_to_all(velocity, 'col', split_axis=1, concat_axis=2, tiled=True)]
    transpose x0 -> x1, local copies, waits for them, and re-layouts: none -> 7.04 us  [per_device(): homeward.transpose(2, 4, 0, 3, 5, 1)]
    all_to_all x4 -> x0, local copies, waits for them, and re-layouts: 6.58 us -> none  [the longest x1 1.97 us: per_device(): lax.all_to_all(span_term, 'col', split_axis=2, concat_axis=1, tiled=True)]
    another operation x1 -> x0, local copies, waits for them, and re-layouts: 4.39 us -> none  [per_device(): span_term = jnp.stack(span_terms, axis=1)]
  transfers between devices with their start and end apart: 4 -> 0, of which waited for: 4 -> 0; matrix products, arithmetic and copies ran while one was open for 11% -> 0% of each run, Pallas kernels for 0% -> 0%
where the time goes in v2:
time: 317 us; the launch traced here: 315 us
  blocking collectives  192 us (61%)
  local copies, waits for them, and re-layouts  111 us (35%)
  other arithmetic  6.69 us (2%)
  matrix products  5.51 us (2%)
    all_to_all x1, blocking collectives, per_device(): lax.all_to_all(outgoing, ('row', 'col'), split_axis=0, concat_axis=0, til...  104 us
    all_to_all x1, blocking collectives, per_device(): lax.all_to_all(homeward, ('row', 'col'), split_axis=0, concat_axis=0, til...  88.2 us
    unnamed x18, local copies, waits for them, and re-layouts  52.1 us
    reshape x2, local copies, waits for them, and re-layouts, per_device(): back.transpose(1, 2, 3, 0, 4)  14.9 us
    reshape x1, local copies, waits for them, and re-layouts, per_device(): planes.reshape(row_count, column_count, comps, wall_local, span_local, st...  12.7 us
    reshape x1, local copies, waits for them, and re-layouts  8.37 us
    reshape x1, local copies, waits for them, and re-layouts, per_device(): summed.reshape(comps, stream_share, row_count, wall_local, column_count,...  7.96 us
    transpose x1, local copies, waits for them, and re-layouts, per_device(): homeward.transpose(2, 4, 0, 3, 5, 1)  7.04 us

profile of v2, /device:TPU:1, one launch (start us, length us, event | category | flops | bytes accessed | tf_op | source)
XLA Modules:
  0.0 315.5 jit_solution(12337792792822427731)
XLA Ops:
  0.0 0.0 copy-start
  0.0 10.3 %copy.20 = bf16[3,32,16,512]{1,2,0,3:T(8,128)(2,1)} copy(bf16[3,32,16,512]{3,2,1,0:T(8,128)(2,1)} %param.5) | data formatting | bytes 3145728 | tf_op args[0]
  10.3 6.5 %bitcast_bitcast_fusion.1 = bf16[512,3,1,16,32]{4,3,2,1,0:T(8,128)(2,1)} fusion(bf16[3,32,16,512]{1,2,0,3:T(8,128)(2,1)} %copy.20), kind=kLoop, calls=%fused_computation.16 | loop fusion | bytes 3145728
  16.8 8.8 %reshape.72 = bf16[512,2,768]{2,1,0:T(2,128)(2,1)S(1)} reshape(bf16[512,3,1,16,32]{4,3,2,1,0:T(8,128)(2,1)} %bitcast_bitcast_fusion.1) | data formatting | bytes 3145728
  25.6 103.7 %all_to_all.10 = bf16[512,2,768]{2,1,0:T(2,128)(2,1)} all-to-all(bf16[512,2,768]{2,1,0:T(2,128)(2,1)S(1)} %reshape.72), channel_id=1, replica_groups=mesh['row'=16,'col'=32] {'row','col'}, dimensions={0} | all-to-all | bytes 3145728 | tf_op jit(solution)/shard_map/all_to_all | solution.py:18
  129.4 8.6 %reshape.73 = bf16[512,3,1,16,32]{4,3,2,1,0:T(8,128)(2,1)} reshape(bf16[512,2,768]{2,1,0:T(2,128)(2,1)} %all_to_all.10) | data formatting | bytes 3145728
  138.0 12.7 %copy.33 = bf16[16,32,3,32,16,1]{3,0,4,1,2,5:T(8,128)(2,1)} copy(bf16[16,32,3,32,16,1]{3,4,2,1,0,5:T(8,128)(2,1)} %bitcast.69) | data formatting | bytes 3145728 | tf_op jit(solution)/shard_map/reshape | solution.py:19
  150.7 8.4 %reshape.61 = bf16[3,512,512]{1,2,0:T(8,128)(2,1)S(1)} reshape(bf16[3,1,16,32,32,16]{3,2,5,4,0,1:T(8,128)(2,1)} %bitcast.67) | data formatting | bytes 3145728 | tf_op jit(solution)/shard_map/reshape
  159.1 6.7 %slice_convert_fusion = (f32[1,1,16,32,32,16]{3,2,5,4,0,1:T(8,128)}, f32[1,1,16,32,32,16]{3,2,5,4,0,1:T(8,128)}) fusion(bf16[3,1,16,32,32,16]{3,2,5,4,0,1:T(8,128)(2,1)} %bitcast.68), kind=kLoop, calls=%fused_computation.7 | loop fusion | flops 524288 | bytes 3145728 | tf_op jit(solution)/shard_map/convert_element_type | solution.py:28
  165.8 3.5 %reshape.66 = f32[512,512]{0,1:T(8,128)S(1)} reshape(f32[1,1,16,32,32,16]{3,2,5,4,0,1:T(8,128)} %get-tuple-element.5) | data formatting | bytes 2097152 | tf_op jit(solution)/shard_map/convert_element_type | solution.py:28
  169.3 4.6 %reshape.65 = f32[512,512]{0,1:T(8,128)} reshape(f32[1,1,16,32,32,16]{3,2,5,4,0,1:T(8,128)} %get-tuple-element.6) | data formatting | bytes 2097152 | tf_op jit(solution)/shard_map/convert_element_type | solution.py:25
  174.0 0.0 copy-done
  174.0 0.0 copy-start.3
  174.0 1.0 fusion.4
  174.9 0.1 copy-done.3
  175.0 0.0 copy-start.2
  175.0 0.0 copy-start.5
  175.0 1.0 fusion.7
  176.0 0.2 copy-done.2
  176.2 0.1 copy-done.5
  176.4 0.0 copy-start.4
  176.4 1.1 fusion.2
  177.5 0.0 copy-done.4
  177.5 2.4 fusion
  179.9 8.0 %reshape.62 = bf16[3,1,16,32,32,16]{3,2,5,4,0,1:T(8,128)(2,1)} reshape(bf16[3,1,512,512]{2,3,0,1:T(8,128)(2,1)} %fusion) | data formatting | bytes 3145728 | tf_op jit(solution)/shard_map/reshape | solution.py:31
  187.8 7.0 %copy.26 = bf16[16,32,3,32,16,1]{3,4,2,1,0,5:T(8,128)(2,1)} copy(bf16[16,32,3,32,16,1]{3,0,4,1,2,5:T(8,128)(2,1)} %bitcast.70) | data formatting | bytes 3145728 | tf_op jit(solution)/shard_map/transpose | solution.py:32
  194.9 8.8 %reshape.74 = bf16[512,2,768]{2,1,0:T(2,128)(2,1)S(1)} reshape(bf16[512,3,1,16,32]{4,3,2,1,0:T(8,128)(2,1)} %bitcast.71) | data formatting | bytes 3145728
  203.7 88.2 %all_to_all.11 = bf16[512,2,768]{2,1,0:T(2,128)(2,1)} all-to-all(bf16[512,2,768]{2,1,0:T(2,128)(2,1)S(1)} %reshape.74), channel_id=1, replica_groups=mesh['row'=16,'col'=32] {'row','col'}, dimensions={0} | all-to-all | bytes 3145728 | tf_op jit(solution)/shard_map/all_to_all | solution.py:33
  291.9 8.6 %reshape.75 = bf16[512,3,1,16,32]{4,3,2,1,0:T(8,128)(2,1)} reshape(bf16[512,2,768]{2,1,0:T(2,128)(2,1)} %all_to_all.11) | data formatting | bytes 3145728
  300.6 6.6 %bitcast_bitcast_fusion = bf16[3,32,16,512]{1,2,0,3:T(8,128)(2,1)} fusion(bf16[512,3,1,16,32]{4,3,2,1,0:T(8,128)(2,1)} %reshape.75), kind=kLoop, calls=%fused_computation.15 | loop fusion | bytes 3145728 | tf_op jit(solution)/shard_map/reshape | solution.py:34
  307.1 8.3 %copy.27 = bf16[3,32,16,512]{3,2,1,0:T(8,128)(2,1)} copy(bf16[3,32,16,512]{1,2,0,3:T(8,128)(2,1)} %bitcast_bitcast_fusion) | data formatting | bytes 3145728 | tf_op jit(solution)/shard_map/reshape | solution.py:34
  315.5 0.0 copy-done.1
  (1 shorter events, 0.0 us)
Async XLA Ops:
  0.0 174.0 %copy-start = (bf16[512,512]{1,0:T(8,128)(2,1)S(1)}, bf16[512,512]{1,0:T(8,128)(2,1)}, u32[]{:S(2)}) copy-start(bf16[512,512]{1,0:T(8,128)(2,1)} %param.9) | copy-start | bytes 1572868
  174.0 1.0 copy-start.3
  175.0 1.2 copy-start.2
  175.0 1.4 copy-start.5
  176.4 1.1 copy-start.4
  300.6 14.9 %copy-start.1 = (bf16[512,512]{1,0:T(8,128)(2,1)S(1)}, bf16[512,512]{1,0:T(8,128)(2,1)}, u32[]{:S(2)}) copy-start(bf16[512,512]{1,0:T(8,128)(2,1)} %param.9) | copy-start | bytes 1572868

commit v3 on v1

v3 whole, which is shorter than its diff:
```python
import jax
import jax.numpy as jnp
from jax import lax
from jax.sharding import PartitionSpec as P


def rate_of_change(slope, diffusion, lines, carrier):
    gradient = jnp.einsum("ij,cjm->cim", slope, lines, preferred_element_type=jnp.float32)
    curvature = jnp.einsum("ij,cjm->cim", diffusion, lines, preferred_element_type=jnp.float32)
    term = curvature - carrier[None].astype(jnp.float32) * gradient
    return term.astype(jnp.bfloat16)


def exchange(blocks, axis):
    return lax.all_to_all(blocks, axis, split_axis=0, concat_axis=0, tiled=True)


def per_device(velocity, wall_slope, wall_diffusion, span_slope, span_diffusion):
    row_count = lax.axis_size("row")
    column_count = lax.axis_size("col")
    comps, wall_local, span_local, stream_len = velocity.shape
    wall_total = wall_local * row_count
    span_total = span_local * column_count
    zr = span_local // row_count
    ws = wall_local // column_count

    send = velocity.reshape(comps, wall_local, row_count, zr, stream_len).transpose(2, 0, 3, 1, 4)
    got = exchange(send, "row")
    wall_lines = got.transpose(1, 2, 0, 3, 4).reshape(comps, zr, wall_total, stream_len)
    wall_parts = []
    for k in range(zr):
        lines = wall_lines[:, k]
        wall_parts.append(rate_of_change(wall_slope, wall_diffusion, lines, lines[1]))
    wall_term = jnp.stack(wall_parts, axis=1)
    send = wall_term.reshape(comps, zr, row_count, wall_local, stream_len).transpose(2, 0, 1, 3, 4)
    wall_back = exchange(send, "row")
    wall_back = wall_back.transpose(1, 3, 0, 2, 4).reshape(comps, wall_local, span_local, stream_len)

    send = velocity.reshape(comps, column_count, ws, span_local, stream_len).transpose(1, 0, 2, 3, 4)
    got = exchange(send, "col")
    span_lines = got.transpose(1, 2, 0, 3, 4).reshape(comps, ws, span_total, stream_len)
    span_parts = []
    for k in range(ws):
        lines = span_lines[:, k]
        span_parts.append(rate_of_change(span_slope, span_diffusion, lines, lines[2]))
    span_term = jnp.stack(span_parts, axis=1)
    send = span_term.reshape(comps, ws, column_count, span_local, stream_len).transpose(2, 0, 1, 3, 4)
    span_back = exchange(send, "col")
    span_back = span_back.transpose(1, 0, 2, 3, 4).reshape(comps, wall_local, span_local, stream_len)

    summed = wall_back.astype(jnp.float32) + span_back.astype(jnp.float32)
    return summed.astype(jnp.bfloat16)


def solution(mesh):
    in_specs = (P(None, "row", "col", None), P(), P(), P(), P())
    out_specs = P(None, "row", "col", None)
    return jax.shard_map(
        per_device, mesh=mesh, in_specs=in_specs, out_specs=out_specs, check_vma=False
    )
```

time: 270 us -> 241 us (0.89)
  blocking collectives: 0 us -> 82.7 us
  waiting for transfers between devices: 190 us -> 108 us
  local copies, waits for them, and re-layouts: 28.6 us -> 11 us
  starting transfers between devices: 37 us -> 30.2 us
  matrix products: 6.65 us -> 3.92 us
    all_to_all x0 -> x1, blocking collectives: none -> 82.7 us  [exchange(): return lax.all_to_all(blocks, axis, split_axis=0, concat_axis=0, tiled=True)]
    all_to_all x4 -> x3, waiting for transfers between devices: 190 us -> 108 us  [exchange(): return lax.all_to_all(blocks, axis, split_axis=0, concat_axis=0, tiled=True)]
    all_to_all x4 -> x3, starting transfers between devices: 37 us -> 30.2 us  [exchange(): return lax.all_to_all(blocks, axis, split_axis=0, concat_axis=0, tiled=True)]
    all_to_all x4 -> x1, local copies, waits for them, and re-layouts: 6.58 us -> 1.58 us  [exchange(): return lax.all_to_all(blocks, axis, split_axis=0, concat_axis=0, tiled=True)]
    reshape x1 -> x0, local copies, waits for them, and re-layouts: 4.39 us -> none  [per_device(): wall_term.reshape(comps, wall_total, span_share, stream_len)]
    convert_element_type x2 -> x0, local copies, waits for them, and re-layouts: 4.1 us -> none  [rate_of_change(): term = curvature - carrier[None].astype(jnp.float32) * gradient]
    another operation x1 -> x2, local copies, waits for them, and re-layouts: 4.39 us -> 1.45 us  [the longest x1 1.33 us: per_device(): wall_term.reshape(comps, zr, row_count, wall_local, stream_len)]
    unnamed x16 -> x12, local copies, waits for them, and re-layouts: 6.03 us -> 5.7 us
  transfers between devices with their start and end apart: 4 -> 3, of which waited for: 4 -> 3; matrix products, arithmetic and copies ran while one was open for 11% -> 4% of each run, Pallas kernels for 0% -> 0%
where the time goes in v3:
time: 241 us; the launch traced here: 239 us
  waiting for transfers between devices  108 us (45%)
  blocking collectives  82.7 us (34%)
  starting transfers between devices  30.2 us (13%)
  local copies, waits for them, and re-layouts  11 us (5%)
  matrix products  3.92 us (2%)
  other arithmetic  2.88 us (1%)
    all_to_all x3, waiting for transfers between devices, exchange(): return lax.all_to_all(blocks, axis, split_axis=0, concat_axis=0, tiled=True)  108 us
    all_to_all x1, blocking collectives, exchange(): return lax.all_to_all(blocks, axis, split_axis=0, concat_axis=0, tiled=True)  82.7 us
    all_to_all x3, starting transfers between devices, exchange(): return lax.all_to_all(blocks, axis, split_axis=0, concat_axis=0, tiled=True)  30.2 us
    unnamed x12, local copies, waits for them, and re-layouts  5.7 us
  transfers between devices with their start and end apart: 3, of which 3 were waited for; matrix products, arithmetic and copies ran while one was open for 4% of the time, Pallas kernels for 0%

profile of v3, /device:TPU:1, one launch (start us, length us, event | category | flops | bytes accessed | tf_op | source)
XLA Modules:
  0.0 238.8 jit_solution(7827147485411831591)
XLA Ops:
  0.0 0.0 copy-start
  0.0 3.5 %copy.28 = bf16[3,32,16,512]{3,1,0,2:T(8,128)(2,1)} copy(bf16[3,32,16,512]{3,2,1,0:T(8,128)(2,1)} %param.5) | data formatting | bytes 3145728 | tf_op args[0]
  3.5 0.0 copy-start.1
  3.5 11.1 %all-to-all-start = ((bf16[16,3,1,32,512]{4,3,2,1,0:T(8,128)(2,1)}), bf16[16,3,1,32,512]{4,3,2,1,0:T(8,128)(2,1)}, u32[]{:S(2)}, u32[]{:S(2)}) async-start(bf16[16,3,1,32,512]{4,3,2,1,0:T(8,128)(2,1)} %bitcast.83), calls=%async_computation | async-start | bytes 3145728 | tf_op jit(solution)/shard_map/all_to_all | solution.py:15
  14.6 0.0 copy-done.1
  14.6 1.3 copy.26
  15.9 20.2 %all-to-all-done = bf16[16,3,1,32,512]{4,3,2,1,0:T(8,128)(2,1)} async-done(((bf16[16,3,1,32,512]{4,3,2,1,0:T(8,128)(2,1)}), bf16[16,3,1,32,512]{4,3,2,1,0:T(8,128)(2,1)}, u32[]{:S(2)}, u32[]{:S(2)}) %all-to-all-start) | async-done | bytes 1572896 | tf_op jit(solution)/shard_map/all_to_all | solution.py:15
  36.1 13.2 %all-to-all-start.2 = ((bf16[32,3,1,16,512]{4,3,1,2,0:T(8,128)(2,1)}), bf16[32,3,1,16,512]{4,3,1,2,0:T(8,128)(2,1)S(1)}, u32[]{:S(2)}, u32[]{:S(2)}) async-start(bf16[32,3,1,16,512]{4,3,1,2,0:T(8,128)(2,1)} %bitcast.81), calls=%async_computation.2 | async-start | bytes 3145728 | tf_op jit(solution)/shard_map/all_to_all | solution.py:15
  49.3 1.6 copy.29
  51.0 0.2 bitcast_convert_fusion.1
  51.1 0.0 copy-done
  51.1 0.0 copy-start.3
  51.1 1.0 fusion.9
  52.1 0.0 copy-done.3
  52.2 1.0 fusion.4
  53.2 1.3 copy.27
  54.5 69.5 %all-to-all-done.2 = bf16[32,3,1,16,512]{4,3,1,2,0:T(8,128)(2,1)S(1)} async-done(((bf16[32,3,1,16,512]{4,3,1,2,0:T(8,128)(2,1)}), bf16[32,3,1,16,512]{4,3,1,2,0:T(8,128)(2,1)S(1)}, u32[]{:S(2)}, u32[]{:S(2)}) %all-to-all-start.2) | async-done | bytes 1572896 | tf_op jit(solution)/shard_map/all_to_all | solution.py:15
  124.0 5.9 %all-to-all-start.1 = ((bf16[16,3,1,32,512]{4,3,1,2,0:T(8,128)(2,1)}), bf16[16,3,1,32,512]{4,3,1,2,0:T(8,128)(2,1)}, u32[]{:S(2)}, u32[]{:S(2)}) async-start(bf16[16,3,1,32,512]{4,3,1,2,0:T(8,128)(2,1)} %bitcast.80), calls=%async_computation.1 | async-start | bytes 3145728 | tf_op jit(solution)/shard_map/all_to_all | solution.py:15
  129.9 0.1 copy.14
  130.1 0.0 copy-start.2
  130.1 0.2 bitcast_convert_fusion
  130.3 0.8 copy-done.2
  131.1 0.0 copy-start.4
  131.1 1.0 fusion.6
  132.1 0.1 copy-done.4
  132.2 1.0 fusion.2
  133.2 0.1 copy.25
  133.3 18.2 %all-to-all-done.1 = bf16[16,3,1,32,512]{4,3,1,2,0:T(8,128)(2,1)} async-done(((bf16[16,3,1,32,512]{4,3,1,2,0:T(8,128)(2,1)}), bf16[16,3,1,32,512]{4,3,1,2,0:T(8,128)(2,1)}, u32[]{:S(2)}, u32[]{:S(2)}) %all-to-all-start.1) | async-done | bytes 1572896 | tf_op jit(solution)/shard_map/all_to_all | solution.py:15
  151.5 82.7 %all_to_all.20 = bf16[32,3,1,16,512]{4,3,1,2,0:T(8,128)(2,1)S(1)} all-to-all(bf16[32,3,1,16,512]{4,3,1,2,0:T(8,128)(2,1)S(1)} %bitcast.82), channel_id=1, replica_groups=mesh['row'=16,'col'=32] {'col'}, dimensions={0} | all-to-all | bytes 3145728 | tf_op jit(solution)/shard_map/all_to_all | solution.py:15
  234.2 2.6 %fusion = bf16[3,32,16,512]{3,1,0,2:T(8,128)(2,1)S(1)} fusion(bf16[16,3,1,32,512]{4,3,1,2,0:T(8,128)(2,1)} %all-to-all-done.1, bf16[32,3,1,16,512]{4,3,1,2,0:T(8,128)(2,1)S(1)} %all_to_all.20), kind=kLoop, calls=%fused_computation.1 | loop fusion | flops 3145728 | bytes 4718592 | tf_op jit(solution)/shard_map/convert_element_type | solution.py:52
  236.8 2.0 copy.17
  (2 shorter events, 0.1 us)
Async XLA Ops:
  0.0 51.1 %copy-start = (bf16[512,512]{1,0:T(8,128)(2,1)S(1)}, bf16[512,512]{1,0:T(8,128)(2,1)}, u32[]{:S(2)}) copy-start(bf16[512,512]{1,0:T(8,128)(2,1)} %param.7) | copy-start | bytes 1572868
  3.5 11.1 %copy-start.1 = (bf16[3,32,16,512]{3,2,1,0:T(8,128)(2,1)S(1)}, bf16[3,32,16,512]{3,2,1,0:T(8,128)(2,1)}, u32[]{:S(2)}) copy-start(bf16[3,32,16,512]{3,2,1,0:T(8,128)(2,1)} %param.5) | copy-start | bytes 4718596
  3.5 32.6 %all-to-all-start = ((bf16[16,3,1,32,512]{4,3,2,1,0:T(8,128)(2,1)}), bf16[16,3,1,32,512]{4,3,2,1,0:T(8,128)(2,1)}, u32[]{:S(2)}, u32[]{:S(2)}) async-start(bf16[16,3,1,32,512]{4,3,2,1,0:T(8,128)(2,1)} %bitcast.83), calls=%async_computation | async-start | bytes 3145728 | tf_op jit(solution)/shard_map/all_to_all | solution.py:15
  36.1 87.9 %all-to-all-start.2 = ((bf16[32,3,1,16,512]{4,3,1,2,0:T(8,128)(2,1)}), bf16[32,3,1,16,512]{4,3,1,2,0:T(8,128)(2,1)S(1)}, u32[]{:S(2)}, u32[]{:S(2)}) async-start(bf16[32,3,1,16,512]{4,3,1,2,0:T(8,128)(2,1)} %bitcast.81), calls=%async_computation.2 | async-start | bytes 3145728 | tf_op jit(solution)/shard_map/all_to_all | solution.py:15
  51.1 1.0 copy-start.3
  124.0 27.5 %all-to-all-start.1 = ((bf16[16,3,1,32,512]{4,3,1,2,0:T(8,128)(2,1)}), bf16[16,3,1,32,512]{4,3,1,2,0:T(8,128)(2,1)}, u32[]{:S(2)}, u32[]{:S(2)}) async-start(bf16[16,3,1,32,512]{4,3,1,2,0:T(8,128)(2,1)} %bitcast.80), calls=%async_computation.1 | async-start | bytes 3145728 | tf_op jit(solution)/shard_map/all_to_all | solution.py:15
  130.1 1.0 copy-start.2
  131.1 1.0 copy-start.4

commit v4 on v2

v4 whole, which is shorter than its diff:
```python
import jax
import jax.numpy as jnp
from jax import lax
from jax.sharding import Mesh, PartitionSpec as P

ROW_PARTS = (("y", 4), ("xl", 2), ("core", 2))
COL_PARTS = (("z", 16), ("xh", 2))
NEAR = ("xl", "core")
FAR = ("y", "z", "xh")


def to_bf16_value(x):
    return lax.reduce_precision(x, exponent_bits=8, mantissa_bits=7)


def exchange(blocks, axes):
    return lax.all_to_all(blocks, axes, split_axis=0, concat_axis=0, tiled=True)


def per_device(velocity, wall_slope, wall_diffusion, span_slope, span_diffusion):
    near = lax.axis_size(NEAR)
    ny = lax.axis_size("y")
    nz = lax.axis_size("z")
    nxh = lax.axis_size("xh")
    far = ny * nz * nxh
    comps, wall_local, span_local, stream_len = velocity.shape
    xa = stream_len // near
    xb = xa // far
    wall_group = wall_local * near
    wall_total = wall_group * ny
    span_total = span_local * nz * nxh
    f32 = jnp.float32

    send = velocity.reshape(comps, wall_local, span_local, near, xa).transpose(3, 0, 1, 2, 4)
    got = exchange(send, NEAR)
    send = got.reshape(near, comps, wall_local, span_local, far, xb).transpose(4, 1, 3, 5, 0, 2)
    send = send.reshape(far, comps, span_local, xb, wall_group)
    got = exchange(send, FAR)
    planes = got.reshape(ny, nz, nxh, comps, span_local, xb, wall_group).transpose(3, 5, 1, 2, 4, 0, 6)
    planes = planes.reshape(comps, xb, span_total, wall_total)

    wall_gradient = jnp.einsum("cxzk,yk->cxzy", planes, wall_slope, preferred_element_type=f32)
    wall_curvature = jnp.einsum("cxzk,yk->cxzy", planes, wall_diffusion, preferred_element_type=f32)
    wall_term = to_bf16_value(wall_curvature - planes[1][None].astype(f32) * wall_gradient)
    span_gradient = jnp.einsum("ij,cxjy->cxiy", span_slope, planes, preferred_element_type=f32)
    span_curvature = jnp.einsum("ij,cxjy->cxiy", span_diffusion, planes, preferred_element_type=f32)
    span_term = to_bf16_value(span_curvature - planes[2][None].astype(f32) * span_gradient)
    summed = (wall_term + span_term).astype(jnp.bfloat16)

    send = summed.reshape(comps, xb, nz, nxh, span_local, ny, wall_group).transpose(5, 2, 3, 0, 4, 1, 6)
    send = send.reshape(far, comps, span_local, xb, wall_group)
    got = exchange(send, FAR)
    send = got.reshape(far, comps, span_local, xb, near, wall_local).transpose(4, 1, 5, 2, 0, 3)
    send = send.reshape(near, comps, wall_local, span_local, xa)
    got = exchange(send, NEAR)
    return got.transpose(1, 2, 3, 0, 4).reshape(comps, wall_local, span_local, stream_len)


def solution(mesh):
    names = tuple(n for n, _ in ROW_PARTS + COL_PARTS)
    sizes = tuple(s for _, s in ROW_PARTS + COL_PARTS)
    fine = Mesh(mesh.devices.reshape(sizes), names)
    rows = tuple(n for n, _ in ROW_PARTS)
    cols = tuple(n for n, _ in COL_PARTS)
    in_specs = (P(None, rows, cols, None), P(), P(), P(), P())
    out_specs = P(None, rows, cols, None)
    return jax.shard_map(
        per_device, mesh=fine, in_specs=in_specs, out_specs=out_specs, check_vma=False
    )
```

time: 317 us -> 261 us (0.82)
  local copies, waits for them, and re-layouts: 111 us -> 23.8 us
  blocking collectives: 192 us -> 230 us
  other arithmetic: 6.69 us -> 1.26 us
    unnamed x18 -> x8, local copies, waits for them, and re-layouts: 52.1 us -> 0.92 us
    all_to_all x2 -> x4, blocking collectives: 192 us -> 230 us  [exchange(): return lax.all_to_all(blocks, axes, split_axis=0, concat_axis=0, tiled=True)]
    reshape x5 -> x7, local copies, waits for them, and re-layouts: 44 us -> 13 us  [the longest x2 2.62 us: per_device(): summed.reshape(comps, xb, nz, nxh, span_local, ny, wall_group)]
    convert_element_type x1, other arithmetic: 6.69 us -> 1.26 us  [per_device(): planes[1][None].astype(f32) * wall_gradient]
    transpose x1 -> x3, local copies, waits for them, and re-layouts: 7.04 us -> 4.65 us  [the longest x1 3.17 us: per_device(): got.reshape(ny, nz, nxh, comps, span_local, xb, wall_group)]
where the time goes in v4:
time: 261 us
  blocking collectives  230 us (88%)
  local copies, waits for them, and re-layouts  23.8 us (9%)
  matrix products  5.58 us (2%)
    all_to_all x4, blocking collectives, exchange(): return lax.all_to_all(blocks, axes, split_axis=0, concat_axis=0, tiled=True)  230 us

profile of v4, /device:TPU:1, one launch (start us, length us, event | category | flops | bytes accessed | tf_op | source)
XLA Modules:
  0.0 260.9 jit_solution(7247320174062050838)
XLA Ops:
  0.0 0.0 copy-start
  0.0 2.4 reshape.69
  2.4 0.3 copy.30
  2.7 28.3 %all_to_all.20 = bf16[4,3,32,16,128]{4,3,2,1,0:T(8,128)(2,1)S(1)} all-to-all(bf16[4,3,32,16,128]{4,3,2,1,0:T(8,128)(2,1)S(1)} %copy.30), channel_id=1, replica_groups=mesh['y'=4,'xl'=2,'core'=2,'z'=16,'xh'=2] {'xl','core'}, dimensions={0} | all-to-all | bytes 3145728 | tf_op jit(solution)/shard_map/all_to_all | solution.py:17
  31.0 0.4 copy.31
  31.4 1.7 copy.32
  33.1 91.2 %all_to_all.21 = bf16[128,3,16,1,128]{4,2,1,3,0:T(8,128)(2,1)S(1)} all-to-all(bf16[128,3,16,1,128]{4,2,1,3,0:T(8,128)(2,1)} %copy.32), channel_id=1, replica_groups=mesh['y'=4,'xl'=2,'core'=2,'z'=16,'xh'=2] {'y','z','xh'}, dimensions={0} | all-to-all | bytes 3145728 | tf_op jit(solution)/shard_map/all_to_all | solution.py:17
  124.4 3.2 %copy.33 = bf16[3,1,16,2,16,4,128]{6,5,4,3,2,0,1:T(4,128)(2,1)} copy(bf16[3,1,16,2,16,4,128]{6,4,0,3,2,5,1:T(8,128)(2,1)S(1)} %bitcast.70) | data formatting | bytes 3145728 | tf_op jit(solution)/shard_map/transpose | solution.py:39
  127.5 1.3 slice_convert_fusion.1
  128.8 2.5 reshape.73
  131.3 1.9 copy.34
  133.2 0.7 copy.37
  133.9 0.0 copy-done
  133.9 0.0 copy-start.1
  134.0 1.0 fusion.5
  134.9 0.0 copy-done.1
  135.0 0.0 copy-start.2
  135.0 1.0 fusion.7
  136.0 0.0 copy-done.2
  136.0 1.0 fusion.9
  137.1 0.0 copy-start.3
  137.1 0.2 copy_bitcast_fusion
  137.3 0.9 copy-done.3
  138.1 2.5 fusion.3
  140.7 2.4 reshape.74
  143.0 0.3 copy.40
  143.3 85.0 %all_to_all.22 = bf16[128,3,16,1,128]{4,2,1,3,0:T(8,128)(2,1)S(1)} all-to-all(bf16[128,3,16,1,128]{4,2,1,3,0:T(8,128)(2,1)S(1)} %bitcast.73), channel_id=1, replica_groups=mesh['y'=4,'xl'=2,'core'=2,'z'=16,'xh'=2] {'y','z','xh'}, dimensions={0} | all-to-all | bytes 3145728 | tf_op jit(solution)/shard_map/all_to_all | solution.py:17
  228.3 2.0 copy.42
  230.3 1.8 copy.43
  232.1 25.6 %all_to_all.23 = bf16[4,3,32,16,128]{4,2,3,1,0:T(8,128)(2,1)S(1)} all-to-all(bf16[4,3,32,16,128]{4,2,3,1,0:T(8,128)(2,1)S(1)} %copy.43), channel_id=1, replica_groups=mesh['y'=4,'xl'=2,'core'=2,'z'=16,'xh'=2] {'xl','core'}, dimensions={0} | all-to-all | bytes 3145728 | tf_op jit(solution)/shard_map/all_to_all | solution.py:17
  257.6 1.2 copy.44
  258.9 2.0 reshape.78
Async XLA Ops:
  0.0 133.9 %copy-start = (bf16[512,512]{1,0:T(8,128)(2,1)S(1)}, bf16[512,512]{1,0:T(8,128)(2,1)}, u32[]{:S(2)}) copy-start(bf16[512,512]{1,0:T(8,128)(2,1)} %param.9) | copy-start | bytes 1572868
  133.9 1.0 copy-start.1
  135.0 1.1 copy-start.2
  137.1 1.0 copy-start.3
